TPU v7x, 256 devices: a whole 4x4x8 slice. The times are simulated.
256 devices in a mesh: dp: 8 (over z), tm: 32 (over x, y, core).
Axes of the slice: x: 4, y: 4, z: 8, core: 2. Of those that a mesh axis runs over, the one named last changes fastest.
Arguments:
- clips: bfloat16 [8, 128, 16, 16, 128], P('dp', 'tm'), may hold values from -6 to 6
- segment_ids: int32 [8, 128], P('dp'), may hold values from 0 to 3, never falling along the last dimension, each value on 1 to 64 neighbouring positions
- conv_weight: bfloat16 [3456, 128], replicated, may hold values from -0.109375 to 0.109375
- cotangent: bfloat16 [8, 128, 16, 16, 128], P('dp', 'tm'), may hold values from -6 to 6
Outputs:
- activated: bfloat16 [8, 128, 16, 16, 128], P('dp', 'tm')
- grad_clips: bfloat16 [8, 128, 16, 16, 128], P('dp', 'tm')
- grad_weight: float32 [3456, 128], P('tm')
Inputs may be any that keep to these rules, and one draw needn't show every extreme that they name: segment_ids never fall along a sequence; each clip has 1 to 64 frames and one has exactly that many.
All inputs are finite; a program needn't handle non-finite values.
Results may differ from a plain program's by a relative error of at most 0.013.
Values may be sent and summed in bfloat16 or wider, within the bound.
No kernel may reach another device: no remote copies, remote signals or barrier semaphores. Data moves between devices by JAX's collectives and lax.ppermute only.
A program may use at most 64 MiB of HBM per device.

v0:
```python
import jax
import jax.numpy as jnp
from jax import lax
from jax.sharding import PartitionSpec as P


def from_behind(value, axis, steps):
    count = lax.axis_size(axis)
    leading, last = (max(0, -steps), min(count, count - steps))
    return lax.ppermute(value, axis, [(source, source + steps) for source in range(leading, last)])


def per_device(clips, segment_ids, conv_weight, cotangent):
    nfr = clips.shape[1]
    hh = clips.shape[2]
    ww = clips.shape[3]
    cc = clips.shape[4]
    rows = nfr * hh * ww
    earlier = from_behind(clips[:, nfr - 2 :], "tm", 1)
    extended = jnp.concatenate([earlier, clips], axis=1)[0]
    segrow = segment_ids[0]
    segp = jnp.concatenate([jnp.full((2,), -1, jnp.int32), segrow, jnp.full((2,), -2, jnp.int32)])
    start = lax.axis_index("tm") * nfr
    seglocal = lax.dynamic_slice_in_dim(segp, start, nfr + 4, 0)
    own = seglocal[2 : 2 + nfr]
    patches = []
    pre = jnp.zeros((rows, cc), jnp.float32)
    for kt in range(3):
        moved = extended[kt : kt + nfr]
        keep = seglocal[kt : kt + nfr] == own
        moved = jnp.where(keep[:, None, None, None], moved, jnp.zeros_like(moved))
        padded = jnp.pad(moved, ((0, 0), (1, 1), (1, 1), (0, 0)))
        pieces = [padded[:, ky : ky + hh, kx : kx + ww] for ky in range(3) for kx in range(3)]
        patch = jnp.concatenate(pieces, axis=3).reshape(rows, 9 * cc)
        patches.append(patch)
        pre = pre + jnp.dot(
            patch, conv_weight[kt * 9 * cc : (kt + 1) * 9 * cc], preferred_element_type=jnp.float32
        )
    activated = jax.nn.silu(pre).astype(jnp.bfloat16).reshape(clips.shape)
    sig = jax.nn.sigmoid(pre)
    grad_pre = (
        cotangent.reshape(rows, cc).astype(jnp.float32) * sig * (1.0 + pre * (1.0 - sig))
    ).astype(jnp.bfloat16)
    count = lax.axis_size("dp") * lax.axis_size("tm") * rows
    grad_local = jnp.concatenate(
        [
            lax.dot_general(
                patch, grad_pre, (((0,), (0,)), ((), ())), preferred_element_type=jnp.float32
            )
            for patch in patches
        ],
        axis=0,
    )
    grad_local = grad_local / jnp.sqrt(jnp.float32(count))
    frames_grad = grad_pre.reshape(1, nfr, hh, ww, cc)
    later_part = from_behind(frames_grad[:, :2], "tm", -1)
    grad_ext = jnp.concatenate([frames_grad, later_part], axis=1)[0]
    summed = jnp.zeros((rows, 9 * cc), jnp.float32)
    for kt in range(3):
        d = 2 - kt
        later = grad_ext[d : d + nfr]
        keep = seglocal[2 + d : 2 + d + nfr] == own
        later = jnp.where(keep[:, None, None, None], later, jnp.zeros_like(later)).reshape(rows, cc)
        summed = summed + lax.dot_general(
            later,
            conv_weight[kt * 9 * cc : (kt + 1) * 9 * cc],
            (((1,), (1,)), ((), ())),
            preferred_element_type=jnp.float32,
        )
    summed = summed.reshape(nfr, hh, ww, 9, cc)
    canvas = jnp.zeros((nfr, hh + 2, ww + 2, cc), jnp.float32)
    for ky in range(3):
        for kx in range(3):
            canvas = canvas.at[:, ky : ky + hh, kx : kx + ww].add(summed[:, :, :, ky * 3 + kx])
    grad_clips = canvas[:, 1:-1, 1:-1].astype(jnp.bfloat16).reshape(clips.shape)
    share_rows = grad_local.shape[0] // lax.axis_size("tm")
    total = lax.psum(grad_local, ("dp", "tm"))
    grad_weight = lax.dynamic_slice_in_dim(total, lax.axis_index("tm") * share_rows, share_rows, 0)
    return (activated, grad_clips, grad_weight)


def solution(mesh):
    return jax.shard_map(
        per_device,
        mesh=mesh,
        in_specs=(
            P("dp", "tm", None, None, None),
            P("dp", None),
            P(),
            P("dp", "tm", None, None, None),
        ),
        out_specs=(P("dp", "tm", None, None, None), P("dp", "tm", None, None, None), P("tm", None)),
        check_vma=False,
    )
```

profile of v0, /device:TPU:2, one launch (start us, length us, event | category | flops | bytes accessed | tf_op | source)
XLA Modules:
  0.0 301.6 jit_solution(8584760968547292022)
XLA Ops:
  7.2 0.9 slice.482
  8.2 1.9 collective-permute-start
  11.0 2.5 pad_slice_fusion
  20.5 1.6 fusion.3
  22.9 0.8 fusion.36
  23.7 0.8 fusion.35
  24.6 5.8 %collective-permute-start.1 = (bf16[1,2,16,16,128]{4,3,2,1,0:T(8,128)(2,1)S(1)}, bf16[1,2,16,16,128]{4,3,2,1,0:T(8,128)(2,1)S(1)}, u32[]{:S(2)}, u32[]{:S(2)}) collective-permute-start(bf16[1,2,16,16,128]{4,3,2,1,0:T(8,128)(2,1)S(1)} %slice.545), channel_id=1, source_target_pairs={{1,0},{2,1},{3,2},{4,3},{5,4},{6,5},{7,6},{8,7},{9,8},{10,9},{11,1... | collective-permute-start | bytes 393224 | tf_op jit(solution)/shard_map/ppermute | solution.py:10
  30.4 1.3 maximum_multiply_fusion
  31.7 1.0 collective-permute-done.1
  34.7 3.0 convolution_add_fusion
  37.7 6.9 %reshape.439 = f32[4,16,16,9,128]{4,3,2,1,0:T(8,128)} reshape(f32[1024,1152]{1,0:T(8,128)} %convolution_add_fusion) | data formatting | bytes 9437184 | tf_op jit(solution)/shard_map/reshape | solution.py:70
  44.6 16.6 %fusion.32 = (f32[4,16,16,1,128]{4,3,2,1,0:T(1,128)S(1)}, f32[4,16,16,1,128]{4,3,2,1,0:T(1,128)S(1)}, f32[4,16,16,1,128]{4,3,2,1,0:T(1,128)S(1)}, f32[4,16,16,1,...) fusion(f32[4,16,16,9,128]{4,3,2,1,0:T(8,128)} %reshape.439), kind=kLoop, calls=%fused_computation.101 | loop fusion | bytes 9437184 | tf_op jit(solution)/shard_map/slice | solution.py:74
  61.2 2.2 dynamic-slice_add_fusion
  63.4 4.3 %scatter-add.31 = f32[4,18,18,128]{3,2,1,0:T(8,128)S(1)} dynamic-update-slice(f32[4,18,18,128]{3,2,1,0:T(8,128)S(1)} %scatter-add.30, f32[4,16,16,128]{3,2,1,0:T(8,128)} %dynamic-slice_add_fusion, s32[]{:T(128)} %constant.283.clone.1, s32[]{:T(128)} %bitcast.21, s32[]{:T(128)} %bitcast.22, s32[]{:T(128)} %constant.283.clone.1) | dynamic-update-slice | bytes 1048580 | tf_op jit(solution)/shard_map/scatter-add | solution.py:74
  67.7 3.8 %add_select_fusion = f32[4,16,16,128]{3,2,1,0:T(8,128)} fusion(f32[4,16,16,128]{3,2,1,0:T(8,128)} %bitcast.89, f32[4,18,18,128]{3,2,1,0:T(8,128)S(1)} %scatter-add.31, s32[]{:T(128)} %bitcast.24, s32[]{:T(128)} %bitcast.25, pred[]{:T(512)} %and_reduce_fusion), kind=kLoop, calls=%fused_computation.5 | loop fusion | flops 262144 | bytes 1572873 | tf_op jit(solution)/shard_map/select.11
  71.5 4.3 %scatter-add.34 = f32[4,18,18,128]{3,2,1,0:T(8,128)S(1)} dynamic-update-slice(f32[4,18,18,128]{3,2,1,0:T(8,128)S(1)} %scatter-add.31, f32[4,16,16,128]{3,2,1,0:T(8,128)} %add_select_fusion, s32[]{:T(128)} %constant.283.clone.1, s32[]{:T(128)} %bitcast.24, s32[]{:T(128)} %bitcast.25, s32[]{:T(128)} %constant.283.clone.1) | dynamic-update-slice | bytes 1048580 | tf_op jit(solution)/shard_map/scatter-add | solution.py:74
  75.8 1.1 fusion.1
  77.0 0.9 slice_add_fusion.4
  77.9 3.0 %scatter-add.36 = f32[4,18,18,128]{3,2,1,0:T(8,128)S(1)} dynamic-update-slice(f32[4,18,18,128]{3,2,1,0:T(8,128)S(1)} %fusion.1, f32[4,16,16,128]{3,2,1,0:T(8,128)} %slice_add_fusion.4, s32[]{:T(128)} %constant.283.clone.1, s32[]{:T(128)} %constant.292.clone.1, s32[]{:T(128)} %constant.292.clone.1, s32[]{:T(128)} %constant.283.clone.1) | dynamic-update-slice | bytes 1048580 | tf_op jit(solution)/shard_map/scatter-add | solution.py:74
  81.0 1.7 scatter-add.39
  82.8 1.7 scatter-add.41
  84.6 1.7 scatter-add.44
  87.0 206.2 %all-reduce.6.cloned.1.call-done = f32[3456,128]{1,0:T(8,128)} async-done(((f32[3456,128]{1,0:T(8,128)}), f32[3456,128]{1,0:T(8,128)}) %all-reduce.6.cloned.1.call-update) | async-done | bytes 1769488 | tf_op jit(solution)/shard_map/psum | solution.py:77
  293.3 1.5 constant_dynamic-slice_fusion
  (69 shorter events, 11.6 us)
Async XLA Ops:
  7.2 7.2 %copy-start = (bf16[1,4,16,16,128]{4,3,2,1,0:T(8,128)(2,1)S(1)}, bf16[1,4,16,16,128]{4,3,2,1,0:T(8,128)(2,1)}, u32[]{:S(2)}) copy-start(bf16[1,4,16,16,128]{4,3,2,1,0:T(8,128)(2,1)} %param.22) | copy-start | bytes 786436
  7.2 286.1 %all-reduce.6.cloned.1.call-start = ((), (), s32[]{:S(2)}) async-start(), calls=%async_computation | async-start | bytes 3538944 | tf_op jit(solution)/shard_map/psum | solution.py:77
  8.2 8.4 %collective-permute-start = (bf16[1,2,16,16,128]{4,3,2,1,0:T(8,128)(2,1)S(1)}, bf16[1,2,16,16,128]{4,3,2,1,0:T(8,128)(2,1)S(1)}, u32[]{:S(2)}, u32[]{:S(2)}) collective-permute-start(bf16[1,2,16,16,128]{4,3,2,1,0:T(8,128)(2,1)S(1)} %slice.482), channel_id=1, source_target_pairs={{0,1},{1,2},{2,3},{3,4},{4,5},{5,6},{6,7},{7,8},{8,9},{9,10},{10,1... | collective-permute-start | bytes 393224 | tf_op jit(solution)/shard_map/ppermute | solution.py:10
  13.5 1.2 copy-start.2
  17.6 1.2 copy-start.1
  19.5 1.0 copy-start.3
  24.6 8.1 %collective-permute-start.1 = (bf16[1,2,16,16,128]{4,3,2,1,0:T(8,128)(2,1)S(1)}, bf16[1,2,16,16,128]{4,3,2,1,0:T(8,128)(2,1)S(1)}, u32[]{:S(2)}, u32[]{:S(2)}) collective-permute-start(bf16[1,2,16,16,128]{4,3,2,1,0:T(8,128)(2,1)S(1)} %slice.545), channel_id=1, source_target_pairs={{1,0},{2,1},{3,2},{4,3},{5,4},{6,5},{7,6},{8,7},{9,8},{10,9},{11,1... | collective-permute-start | bytes 393224 | tf_op jit(solution)/shard_map/ppermute | solution.py:10
Sparse Core Ops, SparseCore 0:
  31.9 261.3 all-reduce.5
where the time goes:
time: 302 us
  waiting for transfers between devices  207 us (69%)
  local copies, waits for them, and re-layouts  50.1 us (17%)
  between operations  14.5 us (5%)
  other arithmetic  11.7 us (4%)
  matrix products  10.2 us (3%)
  starting transfers between devices  7.76 us (3%)
    psum x1, waiting for transfers between devices, per_device(): total = lax.psum(grad_local, ('dp', 'tm'))  206 us
    scatter-add x7, local copies, waits for them, and re-layouts, per_device(): canvas.at[:, ky:ky + hh, kx:kx + ww].add(summed[:, :, :, ky * 3 + kx])  16.8 us
    slice x1, local copies, waits for them, and re-layouts, per_device(): summed[:, :, :, ky * 3 + kx]  16.6 us
    ppermute x2, starting transfers between devices, from_behind(): lax.ppermute(value, axis, [(source, source + steps) for source in range(l...  7.72 us
    reshape x1, local copies, waits for them, and re-layouts, per_device(): summed = summed.reshape(nfr, hh, ww, 9, cc)  6.85 us
  transfers between devices with their start and end apart: 3, of which 3 were waited for; matrix products, arithmetic and copies ran while one was open for 20% of the time, Pallas kernels for 0%

commit v1 on v0

--- a/solution.py
+++ b/solution.py
@@ -2,6 +2,12 @@
 import jax.numpy as jnp
 from jax import lax
 from jax.sharding import PartitionSpec as P
+
+
+def get_the_stacks_all(piece_in, mesh_ax, row_axis):
+    for k0 in (mesh_ax, row_axis):
+        piece_in = lax.psum(piece_in, k0)
+    return piece_in
 
 
 def from_behind(value, axis, steps):
@@ -74,7 +80,7 @@
             canvas = canvas.at[:, ky : ky + hh, kx : kx + ww].add(summed[:, :, :, ky * 3 + kx])
     grad_clips = canvas[:, 1:-1, 1:-1].astype(jnp.bfloat16).reshape(clips.shape)
     share_rows = grad_local.shape[0] // lax.axis_size("tm")
-    total = lax.psum(grad_local, ("dp", "tm"))
+    total = get_the_stacks_all(grad_local, "dp", "tm")
     grad_weight = lax.dynamic_slice_in_dim(total, lax.axis_index("tm") * share_rows, share_rows, 0)
     return (activated, grad_clips, grad_weight)
 

time: 302 us -> 241 us (0.80)
  waiting for transfers between devices: 207 us -> 145 us
    psum x1 -> x2, waiting for transfers between devices: 206 us -> 144 us  [get_the_stacks_all(): piece_in = lax.psum(piece_in, k0)]
  transfers between devices with their start and end apart: 3 -> 4, of which waited for: 3 -> 4; matrix products, arithmetic and copies ran while one was open for 20% -> 26% of each run, Pallas kernels for 0% -> 0%
where the time goes in v1:
time: 241 us; the launch traced here: 239 us
  waiting for transfers between devices  145 us (60%)
  local copies, waits for them, and re-layouts  50.1 us (21%)
  between operations  14.5 us (6%)
  other arithmetic  11.7 us (5%)
  matrix products  10.2 us (4%)
  starting transfers between devices  7.8 us (3%)
    psum x2, waiting for transfers between devices, get_the_stacks_all(): piece_in = lax.psum(piece_in, k0)  144 us
    scatter-add x7, local copies, waits for them, and re-layouts, per_device(): canvas.at[:, ky:ky + hh, kx:kx + ww].add(summed[:, :, :, ky * 3 + kx])  16.8 us
    slice x1, local copies, waits for them, and re-layouts, per_device(): summed[:, :, :, ky * 3 + kx]  16.6 us
    ppermute x2, starting transfers between devices, from_behind(): lax.ppermute(value, axis, [(source, source + steps) for source in range(l...  7.54 us
    reshape x1, local copies, waits for them, and re-layouts, per_device(): summed = summed.reshape(nfr, hh, ww, 9, cc)  6.86 us
  transfers between devices with their start and end apart: 4, of which 4 were waited for; matrix products, arithmetic and copies ran while one was open for 26% of the time, Pallas kernels for 0%

profile of v1, /device:TPU:2, one launch (start us, length us, event | category | flops | bytes accessed | tf_op | source)
XLA Modules:
  0.0 239.0 jit_solution(15635994529771364323)
XLA Ops:
  7.2 0.9 slice.482
  8.2 1.9 collective-permute-start
  11.0 2.5 %pad_slice_fusion = (bf16[4,16,16,128]{3,2,1,0:T(8,128)(2,1)S(1)}, bf16[4,16,16,128]{3,2,1,0:T(8,128)(2,1)S(1)}, bf16[4,16,16,128]{3,2,1,0:T(8,128)(2,1)S(1)}, b...) fusion(bf16[4,16,16,128]{3,2,1,0:T(8,128)(2,1)} %bitcast.81), kind=kLoop, calls=%fused_computation.6 | loop fusion | bytes 2359296 | tf_op jit(solution)/shard_map/slice | solution.py:39
  20.5 1.6 fusion.3
  23.7 0.8 fusion.35
  24.6 5.6 %collective-permute-start.1 = (bf16[1,2,16,16,128]{4,3,2,1,0:T(8,128)(2,1)S(1)}, bf16[1,2,16,16,128]{4,3,2,1,0:T(8,128)(2,1)S(1)}, u32[]{:S(2)}, u32[]{:S(2)}) collective-permute-start(bf16[1,2,16,16,128]{4,3,2,1,0:T(8,128)(2,1)S(1)} %slice.545), channel_id=1, source_target_pairs={{1,0},{2,1},{3,2},{4,3},{5,4},{6,5},{7,6},{8,7},{9,8},{10,9},{11,1... | collective-permute-start | bytes 393224 | tf_op jit(solution)/shard_map/ppermute | solution.py:16
  30.2 1.3 maximum_multiply_fusion
  31.8 0.9 collective-permute-done.1
  34.7 3.0 %convolution_add_fusion = f32[1024,1152]{1,0:T(8,128)} fusion(f32[1024,1152]{1,0:T(8,128)S(1)} %convolution_add_fusion.1, bf16[1024,128]{1,0:T(8,128)(2,1)S(1)} %get-tuple-element.120, bf16[3456,128]{1,0:T(8,128)(2,1)S(1)} %copy-done.1), kind=kOutput, calls=%fused_computation | convolution fusion | flops 303169536 | bytes 9994240 | tf_op jit(solution)/shard_map/dot_general | solution.py:70
  37.7 6.9 %reshape.439 = f32[4,16,16,9,128]{4,3,2,1,0:T(8,128)} reshape(f32[1024,1152]{1,0:T(8,128)} %convolution_add_fusion) | data formatting | bytes 9437184 | tf_op jit(solution)/shard_map/reshape | solution.py:76
  44.6 16.6 %fusion.32 = (f32[4,16,16,1,128]{4,3,2,1,0:T(1,128)S(1)}, f32[4,16,16,1,128]{4,3,2,1,0:T(1,128)S(1)}, f32[4,16,16,1,128]{4,3,2,1,0:T(1,128)S(1)}, f32[4,16,16,1,...) fusion(f32[4,16,16,9,128]{4,3,2,1,0:T(8,128)} %reshape.439), kind=kLoop, calls=%fused_computation.101 | loop fusion | bytes 9437184 | tf_op jit(solution)/shard_map/slice | solution.py:80
  61.2 2.2 dynamic-slice_add_fusion
  63.4 4.3 %scatter-add.31 = f32[4,18,18,128]{3,2,1,0:T(8,128)S(1)} dynamic-update-slice(f32[4,18,18,128]{3,2,1,0:T(8,128)S(1)} %scatter-add.30, f32[4,16,16,128]{3,2,1,0:T(8,128)} %dynamic-slice_add_fusion, s32[]{:T(128)} %constant.283.clone.1, s32[]{:T(128)} %bitcast.21, s32[]{:T(128)} %bitcast.22, s32[]{:T(128)} %constant.283.clone.1) | dynamic-update-slice | bytes 1048580 | tf_op jit(solution)/shard_map/scatter-add | solution.py:80
  67.7 3.8 %add_select_fusion = f32[4,16,16,128]{3,2,1,0:T(8,128)} fusion(f32[4,16,16,128]{3,2,1,0:T(8,128)} %bitcast.89, f32[4,18,18,128]{3,2,1,0:T(8,128)S(1)} %scatter-add.31, s32[]{:T(128)} %bitcast.24, s32[]{:T(128)} %bitcast.25, pred[]{:T(512)} %and_reduce_fusion), kind=kLoop, calls=%fused_computation.5 | loop fusion | flops 262144 | bytes 1572873 | tf_op jit(solution)/shard_map/select.11
  71.5 4.3 %scatter-add.34 = f32[4,18,18,128]{3,2,1,0:T(8,128)S(1)} dynamic-update-slice(f32[4,18,18,128]{3,2,1,0:T(8,128)S(1)} %scatter-add.31, f32[4,16,16,128]{3,2,1,0:T(8,128)} %add_select_fusion, s32[]{:T(128)} %constant.283.clone.1, s32[]{:T(128)} %bitcast.24, s32[]{:T(128)} %bitcast.25, s32[]{:T(128)} %constant.283.clone.1) | dynamic-update-slice | bytes 1048580 | tf_op jit(solution)/shard_map/scatter-add | solution.py:80
  75.8 1.1 fusion.1
  77.0 0.9 slice_add_fusion.4
  77.9 3.0 %scatter-add.36 = f32[4,18,18,128]{3,2,1,0:T(8,128)S(1)} dynamic-update-slice(f32[4,18,18,128]{3,2,1,0:T(8,128)S(1)} %fusion.1, f32[4,16,16,128]{3,2,1,0:T(8,128)} %slice_add_fusion.4, s32[]{:T(128)} %constant.283.clone.1, s32[]{:T(128)} %constant.292.clone.1, s32[]{:T(128)} %constant.292.clone.1, s32[]{:T(128)} %constant.283.clone.1) | dynamic-update-slice | bytes 1048580 | tf_op jit(solution)/shard_map/scatter-add | solution.py:80
  81.0 1.7 scatter-add.39
  82.6 29.8 %all-reduce.7.cloned.1.call-done = f32[3456,128]{1,0:T(8,128)} async-done(((f32[3456,128]{1,0:T(8,128)}), f32[3456,128]{1,0:T(8,128)}) %all-reduce.7.cloned.1.call-update) | async-done | bytes 1769488 | tf_op jit(solution)/shard_map/psum | solution.py:9
  112.7 1.7 scatter-add.41
  114.4 1.7 scatter-add.44
  116.9 113.9 %all-reduce.9.cloned.1.call-done = f32[3456,128]{1,0:T(8,128)} async-done(((f32[3456,128]{1,0:T(8,128)}), f32[3456,128]{1,0:T(8,128)}) %all-reduce.9.cloned.1.call-update) | async-done | bytes 1769488 | tf_op jit(solution)/shard_map/psum | solution.py:9
  230.7 1.5 constant_dynamic-slice_fusion
  (72 shorter events, 12.7 us)
Async XLA Ops:
  7.2 7.2 %copy-start = (bf16[1,4,16,16,128]{4,3,2,1,0:T(8,128)(2,1)S(1)}, bf16[1,4,16,16,128]{4,3,2,1,0:T(8,128)(2,1)}, u32[]{:S(2)}) copy-start(bf16[1,4,16,16,128]{4,3,2,1,0:T(8,128)(2,1)} %param.22) | copy-start | bytes 786436
  7.2 105.3 %all-reduce.7.cloned.1.call-start = ((), (), s32[]{:S(2)}) async-start(), calls=%async_computation | async-start | bytes 3538944 | tf_op jit(solution)/shard_map/psum | solution.py:9
  8.2 8.4 %collective-permute-start = (bf16[1,2,16,16,128]{4,3,2,1,0:T(8,128)(2,1)S(1)}, bf16[1,2,16,16,128]{4,3,2,1,0:T(8,128)(2,1)S(1)}, u32[]{:S(2)}, u32[]{:S(2)}) collective-permute-start(bf16[1,2,16,16,128]{4,3,2,1,0:T(8,128)(2,1)S(1)} %slice.482), channel_id=1, source_target_pairs={{0,1},{1,2},{2,3},{3,4},{4,5},{5,6},{6,7},{7,8},{8,9},{9,10},{10,1... | collective-permute-start | bytes 393224 | tf_op jit(solution)/shard_map/ppermute | solution.py:16
  13.5 1.2 copy-start.2
  17.6 1.2 copy-start.1
  19.5 1.0 copy-start.3
  24.6 8.1 %collective-permute-start.1 = (bf16[1,2,16,16,128]{4,3,2,1,0:T(8,128)(2,1)S(1)}, bf16[1,2,16,16,128]{4,3,2,1,0:T(8,128)(2,1)S(1)}, u32[]{:S(2)}, u32[]{:S(2)}) collective-permute-start(bf16[1,2,16,16,128]{4,3,2,1,0:T(8,128)(2,1)S(1)} %slice.545), channel_id=1, source_target_pairs={{1,0},{2,1},{3,2},{4,3},{5,4},{6,5},{7,6},{8,7},{9,8},{10,9},{11,1... | collective-permute-start | bytes 393224 | tf_op jit(solution)/shard_map/ppermute | solution.py:16
  31.6 199.2 %all-reduce.9.cloned.1.call-start = ((), (), s32[]{:S(2)}) async-start(), calls=%async_computation.1 | async-start | bytes 3538944 | tf_op jit(solution)/shard_map/psum | solution.py:9
Sparse Core Ops, SparseCore 0:
  31.7 80.7 all-reduce.6
  115.8 114.8 all-reduce.8
